TPU v7x, 512 devices: a whole 4x8x8 slice. The times are simulated.
512 devices in a mesh: row: 16 (over y, x_lo), col: 16 (over z, core), ka: 2 (over x_hi).
Axes of the slice: x: 4 (x_hi: 2, x_lo: 2; x = x_hi * 2 + x_lo), y: 8, z: 8, core: 2. Of those that a mesh axis runs over, the one named last changes fastest.
Arguments:
- pair: bfloat16 [512, 512, 128], P('row', ('col', 'ka')), may hold values from -6 to 6
- pair_mask: int32 [512, 512], P('row', ('col', 'ka')), may hold values from 0 to 1, as said below
- w_in: bfloat16 [2, 128, 512], replicated, may hold values from -0.5 to 0.5
- w_gate: bfloat16 [2, 128, 128], replicated, may hold values from -0.5 to 0.5
- w_out: bfloat16 [2, 128, 128], replicated, may hold values from -0.5 to 0.5
Outputs:
- updated: bfloat16 [512, 512, 128], P('row', ('col', 'ka'))
Inputs may be any that keep to these rules, and one draw needn't show every extreme that they name: pair_mask[i, j] = v[i] v[j] for a per-token 0/1 validity v; within each aligned run of 16 tokens the real tokens come first and there is at least one.
All inputs are finite; a program needn't handle non-finite values.
Results may differ from a plain program's by a relative error of at most 0.014.
Values may be sent and summed in bfloat16 or wider, within the bound.
No kernel may reach another device: no remote copies, remote signals or barrier semaphores. Data moves between devices by JAX's collectives and lax.ppermute only.
A program may use at most 64 MiB of HBM per device.

v0:
```python
import jax
import jax.numpy as jnp
from jax import lax
from jax.sharding import PartitionSpec as P


def layer_norm(value):
    mean = jnp.mean(value, axis=-1, keepdims=True)
    centred = value - mean
    var = jnp.mean(centred * centred, axis=-1, keepdims=True)
    return centred / jnp.sqrt(var + 1e-05)


def prepare(pair, valid, weight_in, weight_gate):
    normed = layer_norm(pair.astype(jnp.float32)).astype(jnp.bfloat16)
    proj = jnp.einsum("ijc,cd->ijd", normed, weight_in, preferred_element_type=jnp.float32)
    width = proj.shape[-1] // 4
    left = (jax.nn.sigmoid(proj[..., :width]) * proj[..., width : 2 * width] * valid).astype(
        jnp.bfloat16
    )
    right = (
        jax.nn.sigmoid(proj[..., 2 * width : 3 * width]) * proj[..., 3 * width :] * valid
    ).astype(jnp.bfloat16)
    gate = jax.nn.sigmoid(
        jnp.einsum("ijc,cd->ijd", normed, weight_gate, preferred_element_type=jnp.float32)
    )
    return (left, right, gate)


def finish(pair, tri, gate, weight_out):
    normed = layer_norm(tri).astype(jnp.bfloat16)
    proj = jnp.einsum("ijc,cd->ijd", normed, weight_out, preferred_element_type=jnp.float32)
    return (pair.astype(jnp.float32) + gate * proj).astype(jnp.bfloat16)


def transpose_tiles(value, n):
    perm = [(r * n + c, c * n + r) for r in range(n) for c in range(n)]
    return lax.ppermute(value, ("row", "col"), perm)


def on_device(n, pair, pair_mask, w_in, w_gate, w_out):
    valid = pair_mask.astype(jnp.float32)[..., None]
    left, right, gate = prepare(pair, valid, w_in[0], w_gate[0])
    left_rows = lax.all_gather(left, "col", axis=1, tiled=True)
    right_diag = lax.all_gather(transpose_tiles(right, n), "row", axis=1, tiled=True)
    partial_value = jnp.einsum(
        "ikc,jkc->ijc", left_rows, right_diag, preferred_element_type=jnp.float32
    )
    tri = lax.psum_scatter(
        partial_value.astype(jnp.bfloat16), "ka", scatter_dimension=1, tiled=True
    ).astype(jnp.float32)
    middle = finish(pair, tri, gate, w_out[0])
    left, right, gate = prepare(middle, valid, w_in[1], w_gate[1])
    right_cols = lax.all_gather(right, "row", axis=0, tiled=True)
    left_half = lax.all_gather(transpose_tiles(left, n), "col", axis=0, tiled=True)
    left_diag = lax.all_gather(left_half, "ka", axis=1, tiled=True)
    tri = jnp.einsum("kic,kjc->ijc", left_diag, right_cols, preferred_element_type=jnp.float32)
    return finish(middle, tri, gate, w_out[1])


def solution(mesh):
    n = mesh.shape["row"]
    assert mesh.shape["col"] == n
    placed = (P("row", ("col", "ka"), None), P("row", ("col", "ka")), P(), P(), P())
    return jax.shard_map(
        lambda *a: on_device(n, *a),
        mesh=mesh,
        in_specs=placed,
        out_specs=P("row", ("col", "ka"), None),
        check_vma=False,
    )
```

profile of v0, /device:TPU:1, one launch (start us, length us, event | category | flops | bytes accessed | tf_op | source)
XLA Modules:
  0.0 423.1 jit_solution(14155994391619889289)
XLA Ops:
  6.5 1.0 convert_reduce_fusion.1
  7.7 1.1 fusion.18
  9.1 0.7 convert_element_type.52
  9.8 1.3 fusion.42
  11.2 0.8 fusion.31
  12.1 4.5 %collective-permute-start = (bf16[32,16,128]{2,1,0:T(8,128)(2,1)S(1)}, bf16[32,16,128]{2,1,0:T(8,128)(2,1)S(1)}, u32[]{:S(2)}, u32[]{:S(2)}) collective-permute-start(bf16[32,16,128]{2,1,0:T(8,128)(2,1)S(1)} %get-tuple-element.8), channel_id=1, source_target_pairs={{0,0},{2,32},{4,64},{6,96},{8,128},{10,160},{12,192},{14,224},{16,... | collective-permute-start | bytes 393224 | tf_op jit(solution)/shard_map/ppermute | solution.py:38
  16.6 2.6 collective-permute-done
  19.2 0.6 copy-done.3
  19.9 45.1 %all-gather.8.cloned.1.call-done = bf16[32,256,128]{2,1,0:T(8,128)(2,1)} async-done(((bf16[32,16,128]{2,1,0:T(8,128)(2,1)}), bf16[32,256,128]{2,1,0:T(8,128)(2,1)}) %all-gather.8.cloned.1.call-update) | async-done | bytes 2097168 | tf_op jit(solution)/shard_map/all_gather | solution.py:44
  65.1 15.2 %copy.49 = bf16[32,256,128]{0,1,2:T(8,128)(2,1)} copy(bf16[32,256,128]{2,1,0:T(8,128)(2,1)} %all-gather.8.cloned.1.call-done) | data formatting | bytes 4194304 | tf_op jit(solution)/shard_map/all_gather | solution.py:44
  80.3 57.6 %all-gather.6.cloned.1.call-done = bf16[32,256,128]{2,1,0:T(8,128)(2,1)} async-done(((bf16[32,16,128]{2,1,0:T(8,128)(2,1)}), bf16[32,256,128]{2,1,0:T(8,128)(2,1)}) %all-gather.6.cloned.1.call-update) | async-done | bytes 2097168 | tf_op jit(solution)/shard_map/all_gather | solution.py:45
  137.9 15.2 %copy.48 = bf16[32,256,128]{0,1,2:T(8,128)(2,1)} copy(bf16[32,256,128]{2,1,0:T(8,128)(2,1)} %all-gather.6.cloned.1.call-done) | data formatting | bytes 4194304 | tf_op jit(solution)/shard_map/all_gather | solution.py:45
  153.2 9.2 %fusion = bf16[32,32,128]{0,1,2:T(8,128)(2,1)} fusion(bf16[32,256,128]{0,1,2:T(8,128)(2,1)} %copy.48, bf16[32,256,128]{0,1,2:T(8,128)(2,1)} %copy.49), kind=kOutput, calls=%fused_computation.1 | convolution fusion | flops 67239936 | bytes 4456448 | tf_op jit(solution)/shard_map/ikc,jkc->ijc/dot_general | solution.py:46
  162.8 39.5 %reduce-scatter.2.cloned.1.call-done = bf16[32,16,128]{0,1,2:T(8,128)(2,1)} async-done(((bf16[32,32,128]{0,1,2:T(8,128)(2,1)}), bf16[32,16,128]{0,1,2:T(8,128)(2,1)}) %reduce-scatter.2.cloned.1.call-update) | async-done | bytes 131088 | tf_op jit(solution)/shard_map/reduce_scatter | solution.py:49
  202.3 1.2 convert_reduce_fusion
  203.5 1.3 fusion.14
  204.8 1.2 fusion.15
  206.0 0.5 copy.50
  207.3 0.4 fusion.40
  207.7 0.8 fusion.21
  208.5 2.9 collective-permute-start.1
  211.4 3.4 collective-permute-done.1
  214.8 0.6 copy-done.2
  215.5 0.5 all-gather.10.cloned.1.call-update
  216.1 53.4 %all-gather.12.cloned.1.call-done = bf16[512,16,128]{2,1,0:T(8,128)(2,1)} async-done(((bf16[32,16,128]{2,1,0:T(8,128)(2,1)}), bf16[512,16,128]{2,1,0:T(8,128)(2,1)}) %all-gather.12.cloned.1.call-update) | async-done | bytes 2097168 | tf_op jit(solution)/shard_map/all_gather | solution.py:55
  269.5 4.9 %copy.55 = bf16[512,16,128]{0,1,2:T(8,128)(2,1)} copy(bf16[512,16,128]{2,1,0:T(8,128)(2,1)} %all-gather.12.cloned.1.call-done) | data formatting | bytes 4194304 | tf_op jit(solution)/shard_map/all_gather | solution.py:55
  274.8 59.3 %all-gather.10.cloned.1.call-done = bf16[512,16,128]{2,1,0:T(8,128)(2,1)} async-done(((bf16[32,16,128]{2,1,0:T(8,128)(2,1)}), bf16[512,16,128]{2,1,0:T(8,128)(2,1)}) %all-gather.10.cloned.1.call-update) | async-done | bytes 2097168 | tf_op jit(solution)/shard_map/all_gather | solution.py:54
  334.1 3.9 copy.56
  338.0 73.1 %all-gather.14.cloned.1.call-done = bf16[512,32,128]{0,1,2:T(8,128)(2,1)} async-done(((bf16[512,16,128]{0,1,2:T(8,128)(2,1)}), bf16[512,32,128]{0,1,2:T(8,128)(2,1)}) %all-gather.14.cloned.1.call-update) | async-done | bytes 4194320 | tf_op jit(solution)/shard_map/all_gather | solution.py:56
  411.1 3.4 fusion.57
  414.9 0.5 copy.57
  415.4 0.8 fusion.13
  (44 shorter events, 2.6 us)
Async XLA Ops:
  6.5 58.5 %all-gather.8.cloned.1.call-start = ((), (), s32[]{:S(2)}) async-start(), calls=%async_computation.2 | async-start | bytes 2228224 | tf_op jit(solution)/shard_map/all_gather | solution.py:44
  12.0 125.9 %all-gather.6.cloned.1.call-start = ((), (), s32[]{:S(2)}) async-start(), calls=%async_computation.1 | async-start | bytes 2228224 | tf_op jit(solution)/shard_map/all_gather | solution.py:45
  12.1 7.1 %collective-permute-start = (bf16[32,16,128]{2,1,0:T(8,128)(2,1)S(1)}, bf16[32,16,128]{2,1,0:T(8,128)(2,1)S(1)}, u32[]{:S(2)}, u32[]{:S(2)}) collective-permute-start(bf16[32,16,128]{2,1,0:T(8,128)(2,1)S(1)} %get-tuple-element.8), channel_id=1, source_target_pairs={{0,0},{2,32},{4,64},{6,96},{8,128},{10,160},{12,192},{14,224},{16,... | collective-permute-start | bytes 393224 | tf_op jit(solution)/shard_map/ppermute | solution.py:38
  19.2 0.7 copy-start.3
  19.9 182.4 %reduce-scatter.2.cloned.1.call-start = ((), (), s32[]{:S(2)}) async-start(), calls=%async_computation.3 | async-start | bytes 1572864 | tf_op jit(solution)/shard_map/reduce_scatter | solution.py:49
  153.2 9.3 %copy-start = (bf16[32,16,128]{2,1,0:T(8,128)(2,1)S(1)}, bf16[32,16,128]{2,1,0:T(8,128)(2,1)}, u32[]{:S(2)}) copy-start(bf16[32,16,128]{2,1,0:T(8,128)(2,1)} %param.5) | copy-start | bytes 393220
  153.2 9.3 %copy-start.5 = (bf16[2,128,128]{2,1,0:T(8,128)(2,1)S(1)}, bf16[2,128,128]{2,1,0:T(8,128)(2,1)}, u32[]{:S(2)}) copy-start(bf16[2,128,128]{2,1,0:T(8,128)(2,1)} %param.8) | copy-start | bytes 196612
  162.3 44.1 %copy-start.4 = (bf16[2,128,128]{2,1,0:T(8,128)(2,1)S(1)}, bf16[2,128,128]{2,1,0:T(8,128)(2,1)}, u32[]{:S(2)}) copy-start(bf16[2,128,128]{2,1,0:T(8,128)(2,1)} %param.9) | copy-start | bytes 196612
  162.3 45.0 %copy-start.1 = (bf16[2,128,512]{2,1,0:T(8,128)(2,1)S(1)}, bf16[2,128,512]{2,1,0:T(8,128)(2,1)}, u32[]{:S(2)}) copy-start(bf16[2,128,512]{2,1,0:T(8,128)(2,1)} %param.7) | copy-start | bytes 786436
  162.4 107.2 %all-gather.12.cloned.1.call-start = ((), (), s32[]{:S(2)}) async-start(), calls=%async_computation.5 | async-start | bytes 2228224 | tf_op jit(solution)/shard_map/all_gather | solution.py:55
  208.5 6.3 %collective-permute-start.1 = (bf16[32,16,128]{2,1,0:T(8,128)(2,1)S(1)}, bf16[32,16,128]{2,1,0:T(8,128)(2,1)S(1)}, u32[]{:S(2)}, u32[]{:S(2)}) collective-permute-start(bf16[32,16,128]{2,1,0:T(8,128)(2,1)S(1)} %get-tuple-element.5), channel_id=1, source_target_pairs={{0,0},{2,32},{4,64},{6,96},{8,128},{10,160},{12,192},{14,224},{16,... | collective-permute-start | bytes 393224 | tf_op jit(solution)/shard_map/ppermute | solution.py:38
  214.8 0.6 copy-start.2
  215.5 118.6 %all-gather.10.cloned.1.call-start = ((), (), s32[]{:S(2)}) async-start(), calls=%async_computation.4 | async-start | bytes 2228224 | tf_op jit(solution)/shard_map/all_gather | solution.py:54
  216.1 195.1 %all-gather.14.cloned.1.call-start = ((), (), s32[]{:S(2)}) async-start(), calls=%async_computation.6 | async-start | bytes 6291456 | tf_op jit(solution)/shard_map/all_gather | solution.py:56
Sparse Core Ops, SparseCore 0:
  12.1 52.8 all-gather.7
  67.1 70.8 all-gather.5
  162.5 39.7 reduce-scatter.1
  215.6 53.8 all-gather.11
  271.5 62.6 all-gather.9
  336.1 75.0 all-gather.13
where the time goes:
time: 424 us; the launch traced here: 423 us
  waiting for transfers between devices  335 us (79%)
  local copies, waits for them, and re-layouts  42.3 us (10%)
  matrix products  16 us (4%)
  between operations  13.6 us (3%)
  other arithmetic  8.84 us (2%)
  starting transfers between devices  7.61 us (2%)
    all_gather x1, waiting for transfers between devices, on_device(): left_diag = lax.all_gather(left_half, 'ka', axis=1, tiled=True)  73.1 us
    all_gather x1, waiting for transfers between devices, on_device(): right_cols = lax.all_gather(right, 'row', axis=0, tiled=True)  59.3 us
    all_gather x1, waiting for transfers between devices, on_device(): lax.all_gather(transpose_tiles(right, n), 'row', axis=1, tiled=True)  57.6 us
    all_gather x1, waiting for transfers between devices, on_device(): lax.all_gather(transpose_tiles(left, n), 'col', axis=0, tiled=True)  53.4 us
    all_gather x1, waiting for transfers between devices, on_device(): left_rows = lax.all_gather(left, 'col', axis=1, tiled=True)  45.1 us
    reduce_scatter x1, waiting for transfers between devices, on_device(): lax.psum_scatter(partial_value.astype(jnp.bfloat16), 'ka', scatter_dimens...  39.5 us
    all_gather x1, local copies, waits for them, and re-layouts, on_device(): left_rows = lax.all_gather(left, 'col', axis=1, tiled=True)  15.2 us
    all_gather x1, local copies, waits for them, and re-layouts, on_device(): lax.all_gather(transpose_tiles(right, n), 'row', axis=1, tiled=True)  15.2 us
  transfers between devices with their start and end apart: 8, of which 8 were waited for; matrix products, arithmetic and copies ran while one was open for 6% of the time, Pallas kernels for 0%

commit v1 on v0

--- a/solution.py
+++ b/solution.py
@@ -41,7 +41,8 @@
 def on_device(n, pair, pair_mask, w_in, w_gate, w_out):
     valid = pair_mask.astype(jnp.float32)[..., None]
     left, right, gate = prepare(pair, valid, w_in[0], w_gate[0])
-    left_rows = lax.all_gather(left, "col", axis=1, tiled=True)
+    outgoing = jnp.stack([left] * lax.axis_size("col"))
+    left_rows = jnp.concatenate(lax.all_to_all(outgoing, "col", 0, 0), axis=1)
     right_diag = lax.all_gather(transpose_tiles(right, n), "row", axis=1, tiled=True)
     partial_value = jnp.einsum(
         "ikc,jkc->ijc", left_rows, right_diag, preferred_element_type=jnp.float32

time: 424 us -> 394 us (0.929)
  waiting for transfers between devices: 335 us -> 305 us
  starting transfers between devices: 7.61 us -> 19.6 us
  local copies, waits for them, and re-layouts: 42.3 us -> 34.1 us
    all_to_all x0 -> x1, waiting for transfers between devices: none -> 50.9 us  [on_device(): left_rows = jnp.concatenate(lax.all_to_all(outgoing, 'col', 0, 0), axis=1)]
    all_gather x1 -> x0, waiting for transfers between devices: 45.1 us -> none  [on_device(): left_rows = lax.all_gather(left, 'col', axis=1, tiled=True)]
    all_gather x1, waiting for transfers between devices: 57.6 us -> 26 us  [on_device(): lax.all_gather(transpose_tiles(right, n), 'row', axis=1, tiled=True)]
    all_gather x1 -> x0, local copies, waits for them, and re-layouts: 15.2 us -> none  [on_device(): left_rows = lax.all_gather(left, 'col', axis=1, tiled=True)]
    all_to_all x0 -> x1, starting transfers between devices: none -> 12 us  [on_device(): left_rows = jnp.concatenate(lax.all_to_all(outgoing, 'col', 0, 0), axis=1)]
  transfers between devices with their start and end apart: 8 -> 8, of which waited for: 8 -> 7; matrix products, arithmetic and copies ran while one was open for 6% -> 4% of each run, Pallas kernels for 0% -> 0%
where the time goes in v1:
time: 394 us
  waiting for transfers between devices  305 us (77%)
  local copies, waits for them, and re-layouts  34.1 us (9%)
  starting transfers between devices  19.6 us (5%)
  matrix products  13.7 us (3%)
  between operations  13.3 us (3%)
  other arithmetic  8.18 us (2%)
    all_gather x1, waiting for transfers between devices, on_device(): left_diag = lax.all_gather(left_half, 'ka', axis=1, tiled=True)  73.1 us
    all_gather x1, waiting for transfers between devices, on_device(): right_cols = lax.all_gather(right, 'row', axis=0, tiled=True)  59.3 us
    all_gather x1, waiting for transfers between devices, on_device(): lax.all_gather(transpose_tiles(left, n), 'col', axis=0, tiled=True)  53.5 us
    all_to_all x1, waiting for transfers between devices, on_device(): left_rows = jnp.concatenate(lax.all_to_all(outgoing, 'col', 0, 0), axis=1)  50.9 us
    reduce_scatter x1, waiting for transfers between devices, on_device(): lax.psum_scatter(partial_value.astype(jnp.bfloat16), 'ka', scatter_dimens...  37.9 us
    all_gather x1, waiting for transfers between devices, on_device(): lax.all_gather(transpose_tiles(right, n), 'row', axis=1, tiled=True)  26 us
    all_gather x1, local copies, waits for them, and re-layouts, on_device(): lax.all_gather(transpose_tiles(right, n), 'row', axis=1, tiled=True)  15.2 us
    all_to_all x1, starting transfers between devices, on_device(): left_rows = jnp.concatenate(lax.all_to_all(outgoing, 'col', 0, 0), axis=1)  12 us
  transfers between devices with their start and end apart: 8, of which 7 were waited for; matrix products, arithmetic and copies ran while one was open for 4% of the time, Pallas kernels for 0%

profile of v1, /device:TPU:1, one launch (start us, length us, event | category | flops | bytes accessed | tf_op | source)
XLA Modules:
  0.0 393.6 jit_solution(10176634348250687206)
XLA Ops:
  6.5 1.0 convert_reduce_fusion.1
  7.7 1.1 fusion.18
  9.1 0.7 convert_element_type.52
  9.8 1.3 fusion.42
  11.3 4.5 %collective-permute-start = (bf16[32,16,128]{2,1,0:T(8,128)(2,1)S(1)}, bf16[32,16,128]{2,1,0:T(8,128)(2,1)S(1)}, u32[]{:S(2)}, u32[]{:S(2)}) collective-permute-start(bf16[32,16,128]{2,1,0:T(8,128)(2,1)S(1)} %get-tuple-element.8), channel_id=1, source_target_pairs={{0,0},{2,32},{4,64},{6,96},{8,128},{10,160},{12,192},{14,224},{16,... | collective-permute-start | bytes 393224 | tf_op jit(solution)/shard_map/ppermute | solution.py:38
  15.8 1.7 stack.2
  17.6 12.0 %all-to-all-start = ((bf16[16,32,16,128]{3,2,1,0:T(8,128)(2,1)}), bf16[16,32,16,128]{3,2,1,0:T(8,128)(2,1)S(1)}, u32[]{:S(2)}, u32[]{:S(2)}) async-start(bf16[16,32,16,128]{3,2,1,0:T(8,128)(2,1)} %stack.2), calls=%async_computation | async-start | bytes 4194304 | tf_op jit(solution)/shard_map/all_to_all | solution.py:45
  29.7 0.6 copy-done.2
  30.4 50.9 %all-to-all-done = bf16[16,32,16,128]{3,2,1,0:T(8,128)(2,1)S(1)} async-done(((bf16[16,32,16,128]{3,2,1,0:T(8,128)(2,1)}), bf16[16,32,16,128]{3,2,1,0:T(8,128)(2,1)S(1)}, u32[]{:S(2)}, u32[]{:S(2)}) %all-to-all-start) | async-done | bytes 2097184 | tf_op jit(solution)/shard_map/all_to_all | solution.py:45
  81.3 1.9 copy.61
  83.2 3.4 copy.63
  86.6 26.0 %all-gather.5.cloned.1.call-done = bf16[32,256,128]{2,1,0:T(8,128)(2,1)} async-done(((bf16[32,16,128]{2,1,0:T(8,128)(2,1)}), bf16[32,256,128]{2,1,0:T(8,128)(2,1)}) %all-gather.5.cloned.1.call-update) | async-done | bytes 2097168 | tf_op jit(solution)/shard_map/all_gather | solution.py:46
  112.7 15.2 %copy.62 = bf16[32,256,128]{0,1,2:T(8,128)(2,1)} copy(bf16[32,256,128]{2,1,0:T(8,128)(2,1)} %all-gather.5.cloned.1.call-done) | data formatting | bytes 4194304 | tf_op jit(solution)/shard_map/all_gather | solution.py:46
  127.9 6.8 %fusion = bf16[32,32,128]{0,1,2:T(8,128)(2,1)} fusion(bf16[32,256,128]{0,1,2:T(8,128)(2,1)} %copy.62, bf16[32,256,128]{1,0,2:T(8,128)(2,1)S(1)} %copy.63), kind=kOutput, calls=%fused_computation.1 | convolution fusion | flops 67239936 | bytes 4456448 | tf_op jit(solution)/shard_map/ikc,jkc->ijc/dot_general | solution.py:47
  135.2 37.9 %reduce-scatter.2.cloned.1.call-done = bf16[32,16,128]{0,1,2:T(8,128)(2,1)} async-done(((bf16[32,32,128]{0,1,2:T(8,128)(2,1)}), bf16[32,16,128]{0,1,2:T(8,128)(2,1)}) %reduce-scatter.2.cloned.1.call-update) | async-done | bytes 131088 | tf_op jit(solution)/shard_map/reduce_scatter | solution.py:50
  173.1 1.2 convert_reduce_fusion
  174.3 1.3 fusion.14
  175.5 1.2 fusion.15
  176.7 0.5 copy.64
  178.5 0.8 fusion.21
  179.3 2.9 collective-permute-start.1
  182.2 3.4 collective-permute-done.1
  185.6 0.7 copy-done.3
  186.3 0.5 all-gather.7.cloned.1.call-update
  186.9 53.5 %all-gather.9.cloned.1.call-done = bf16[512,16,128]{2,1,0:T(8,128)(2,1)} async-done(((bf16[32,16,128]{2,1,0:T(8,128)(2,1)}), bf16[512,16,128]{2,1,0:T(8,128)(2,1)}) %all-gather.9.cloned.1.call-update) | async-done | bytes 2097168 | tf_op jit(solution)/shard_map/all_gather | solution.py:56
  240.4 4.9 %copy.69 = bf16[512,16,128]{0,1,2:T(8,128)(2,1)} copy(bf16[512,16,128]{2,1,0:T(8,128)(2,1)} %all-gather.9.cloned.1.call-done) | data formatting | bytes 4194304 | tf_op jit(solution)/shard_map/all_gather | solution.py:56
  245.6 59.3 %all-gather.7.cloned.1.call-done = bf16[512,16,128]{2,1,0:T(8,128)(2,1)} async-done(((bf16[32,16,128]{2,1,0:T(8,128)(2,1)}), bf16[512,16,128]{2,1,0:T(8,128)(2,1)}) %all-gather.7.cloned.1.call-update) | async-done | bytes 2097168 | tf_op jit(solution)/shard_map/all_gather | solution.py:55
  304.9 3.9 copy.70
  308.9 73.1 %all-gather.11.cloned.1.call-done = bf16[512,32,128]{0,1,2:T(8,128)(2,1)} async-done(((bf16[512,16,128]{0,1,2:T(8,128)(2,1)}), bf16[512,32,128]{0,1,2:T(8,128)(2,1)}) %all-gather.11.cloned.1.call-update) | async-done | bytes 4194320 | tf_op jit(solution)/shard_map/all_gather | solution.py:57
  382.0 3.4 fusion.57
  385.7 0.5 copy.71
  386.2 0.8 fusion.13
  (45 shorter events, 3.1 us)
Async XLA Ops:
  11.3 18.3 %collective-permute-start = (bf16[32,16,128]{2,1,0:T(8,128)(2,1)S(1)}, bf16[32,16,128]{2,1,0:T(8,128)(2,1)S(1)}, u32[]{:S(2)}, u32[]{:S(2)}) collective-permute-start(bf16[32,16,128]{2,1,0:T(8,128)(2,1)S(1)} %get-tuple-element.8), channel_id=1, source_target_pairs={{0,0},{2,32},{4,64},{6,96},{8,128},{10,160},{12,192},{14,224},{16,... | collective-permute-start | bytes 393224 | tf_op jit(solution)/shard_map/ppermute | solution.py:38
  17.6 63.7 %all-to-all-start = ((bf16[16,32,16,128]{3,2,1,0:T(8,128)(2,1)}), bf16[16,32,16,128]{3,2,1,0:T(8,128)(2,1)S(1)}, u32[]{:S(2)}, u32[]{:S(2)}) async-start(bf16[16,32,16,128]{3,2,1,0:T(8,128)(2,1)} %stack.2), calls=%async_computation | async-start | bytes 4194304 | tf_op jit(solution)/shard_map/all_to_all | solution.py:45
  29.6 83.0 %all-gather.5.cloned.1.call-start = ((), (), s32[]{:S(2)}) async-start(), calls=%async_computation.2 | async-start | bytes 2228224 | tf_op jit(solution)/shard_map/all_gather | solution.py:46
  29.7 0.7 copy-start.2
  30.4 142.7 %reduce-scatter.2.cloned.1.call-start = ((), (), s32[]{:S(2)}) async-start(), calls=%async_computation.3 | async-start | bytes 1572864 | tf_op jit(solution)/shard_map/reduce_scatter | solution.py:50
  127.9 6.9 %copy-start = (bf16[32,16,128]{2,1,0:T(8,128)(2,1)S(1)}, bf16[32,16,128]{2,1,0:T(8,128)(2,1)}, u32[]{:S(2)}) copy-start(bf16[32,16,128]{2,1,0:T(8,128)(2,1)} %param.5) | copy-start | bytes 393220
  127.9 6.9 %copy-start.5 = (bf16[2,128,128]{2,1,0:T(8,128)(2,1)S(1)}, bf16[2,128,128]{2,1,0:T(8,128)(2,1)}, u32[]{:S(2)}) copy-start(bf16[2,128,128]{2,1,0:T(8,128)(2,1)} %param.8) | copy-start | bytes 196612
  134.8 42.5 %copy-start.4 = (bf16[2,128,128]{2,1,0:T(8,128)(2,1)S(1)}, bf16[2,128,128]{2,1,0:T(8,128)(2,1)}, u32[]{:S(2)}) copy-start(bf16[2,128,128]{2,1,0:T(8,128)(2,1)} %param.9) | copy-start | bytes 196612
  134.8 105.6 %all-gather.9.cloned.1.call-start = ((), (), s32[]{:S(2)}) async-start(), calls=%async_computation.5 | async-start | bytes 2228224 | tf_op jit(solution)/shard_map/all_gather | solution.py:56
  135.2 42.9 %copy-start.1 = (bf16[2,128,512]{2,1,0:T(8,128)(2,1)S(1)}, bf16[2,128,512]{2,1,0:T(8,128)(2,1)}, u32[]{:S(2)}) copy-start(bf16[2,128,512]{2,1,0:T(8,128)(2,1)} %param.7) | copy-start | bytes 786436
  179.3 6.3 %collective-permute-start.1 = (bf16[32,16,128]{2,1,0:T(8,128)(2,1)S(1)}, bf16[32,16,128]{2,1,0:T(8,128)(2,1)S(1)}, u32[]{:S(2)}, u32[]{:S(2)}) collective-permute-start(bf16[32,16,128]{2,1,0:T(8,128)(2,1)S(1)} %get-tuple-element.5), channel_id=1, source_target_pairs={{0,0},{2,32},{4,64},{6,96},{8,128},{10,160},{12,192},{14,224},{16,... | collective-permute-start | bytes 393224 | tf_op jit(solution)/shard_map/ppermute | solution.py:38
  185.6 0.7 copy-start.3
  186.3 118.7 %all-gather.7.cloned.1.call-start = ((), (), s32[]{:S(2)}) async-start(), calls=%async_computation.4 | async-start | bytes 2228224 | tf_op jit(solution)/shard_map/all_gather | solution.py:55
  186.8 195.1 %all-gather.11.cloned.1.call-start = ((), (), s32[]{:S(2)}) async-start(), calls=%async_computation.6 | async-start | bytes 6291456 | tf_op jit(solution)/shard_map/all_gather | solution.py:57
Sparse Core Ops, SparseCore 0:
  32.4 80.1 all-gather.4
  134.9 38.1 reduce-scatter.1
  186.4 53.9 all-gather.8
  242.3 62.6 all-gather.6
  306.9 75.0 all-gather.10
